TPU v7x, 128 devices: a whole 4x4x4 slice. The times are simulated.
128 devices in a mesh: ctx: 32 (over x, y, core), head: 4 (over z).
Axes of the slice: x: 4, y: 4, z: 4, core: 2. Of those that a mesh axis runs over, the one named last changes fastest.
Arguments:
- queries: bfloat16 [32768, 4096], P('ctx', 'head'), may hold values from -4.5 to 4.5
- keys: bfloat16 [32768, 4096], P('ctx', 'head'), may hold values from -6 to 6
- values: bfloat16 [32768, 4096], P('ctx', 'head'), may hold values from -5.5 to 5.5
- row_target: int32 [32768], replicated, may hold values from 0 to 32767, as said below
- seg_doc: int32 [32], replicated, may hold values from 0 to 3, as said below
- mem_gate: float32 [32], P('head'), may hold values from -2 to 2
- out_weight: bfloat16 [4096, 4096], P(None, 'head'), may hold values from -0.09375 to 0.09375
Outputs:
- layer_out: bfloat16 [32768, 4096], P('ctx', 'head')
Inputs may be any that keep to these rules, and one draw needn't show every extreme that they name: `row_target`: a permutation of the token indices; the rows of one ctx shard of the loader order hold at most 48 tokens of any one segment, and exactly 48 of some. `seg_doc`: never falling along the segments, every document present with one or more segments.
All inputs are finite; a program needn't handle non-finite values.
Results may differ from a plain program's by a relative error of at most 0.0051.
Values may be sent and summed in bfloat16 or wider, within the bound.
No kernel may reach another device: no remote copies, remote signals or barrier semaphores. Data moves between devices by JAX's collectives and lax.ppermute only.
A program may use at most 128 MiB of HBM per device.

v0:
```python
import jax
import jax.numpy as jnp
from jax import lax
from jax.sharding import PartitionSpec as P


def feature(inputs):
    return jax.nn.elu(inputs) + 1.0


def per_device(queries, keys, values, row_target, seg_doc, mem_gate, out_weight):
    highest = lax.Precision.HIGHEST
    f32, bf16 = (jnp.float32, jnp.bfloat16)
    n = lax.axis_size("ctx")
    me = lax.axis_index("ctx")
    seg, width = queries.shape
    heads = mem_gate.shape[0]
    dh = width // heads
    cap = seg // n + seg // n // 2
    slots = n * cap
    targets = row_target.reshape(n, seg)
    r_idx = jnp.arange(seg, dtype=jnp.int32)
    o_idx = jnp.arange(n, dtype=jnp.int32)
    s_idx = jnp.arange(slots, dtype=jnp.int32)
    w_idx = jnp.arange(cap, dtype=jnp.int32)
    lower = (r_idx[None, :] < r_idx[:, None]).astype(bf16)
    mine = lax.dynamic_index_in_dim(targets, me, 0, keepdims=False)
    owner = mine // seg
    match = (owner[:, None] == o_idx[None, :]).astype(bf16)
    before = jnp.dot(lower, match, preferred_element_type=f32)
    within = jnp.sum(jnp.where(match > 0, before, 0.0), axis=1).astype(jnp.int32)
    send_slot = owner * cap + within
    slot_row = jnp.sum(jnp.where(send_slot[None, :] == s_idx[:, None], r_idx[None, :], 0), axis=1)
    arrived = targets // seg == me
    rank = jnp.dot(arrived.astype(bf16), lower.T, preferred_element_type=f32).astype(jnp.int32)
    hit = arrived[:, None, :] & (rank[:, None, :] == w_idx[None, :, None])
    pslot = jnp.sum(jnp.where(hit, (targets % seg)[:, None, :], 0), axis=2).reshape(slots)
    count = jnp.sum(arrived.astype(jnp.int32), axis=1)
    valid = (w_idx[None, :] < count[:, None]).reshape(slots)
    tok_slot = jnp.sum(
        jnp.where((pslot[None, :] == r_idx[:, None]) & valid[None, :], s_idx[None, :], 0), axis=1
    )
    doc = seg_doc[me]
    start = jnp.min(jnp.where(seg_doc == doc, o_idx, n))
    score_scale = dh ** (-0.5)
    causal = r_idx[:, None] >= r_idx[None, :]
    head_count = lax.axis_size("head")
    out_cols = out_weight.shape[1]
    bounds = [0, heads // 2, heads]
    weight_rows = out_weight.reshape(head_count, heads, dh, out_cols)
    gate_all = jax.nn.sigmoid(mem_gate)
    shifts = []
    step = 1
    while step < n:
        shifts.append(step)
        step *= 2

    def dispatch(source):
        buffer = jnp.take(source, slot_row, axis=0, mode="clip").reshape(n, cap, width)
        got = lax.all_to_all(buffer, "ctx", 0, 0, tiled=True).reshape(slots, width)
        return jnp.take(got, tok_slot, axis=0, mode="clip").reshape(seg, heads, dh)

    key_all = dispatch(keys)
    value_all = dispatch(values)
    query_all = dispatch(queries)

    def local_attention(query_part, key_part, value_part):
        scores = (
            jnp.einsum("qhd,khd->hqk", query_part, key_part, preferred_element_type=f32)
            * score_scale
        )
        scores = jnp.where(causal[None], scores, -1e30)
        row_max = jnp.max(scores, axis=-1, keepdims=True)
        weights = jnp.exp(scores - row_max)
        probabilities = (weights / jnp.sum(weights, axis=-1, keepdims=True)).astype(bf16)
        return jnp.einsum("hqk,khd->qhd", probabilities, value_part, preferred_element_type=f32)

    def one_group(g, hold):
        first, last = (bounds[g], bounds[g + 1])
        group_heads = last - first
        group_width = group_heads * dh
        cuts = [first + round(group_heads * i / len(shifts)) for i in range(len(shifts) + 1)]
        cuts = [c - first for c in cuts]
        key_heads = key_all[:, first:last]
        value_heads = value_all[:, first:last]
        query_heads = query_all[:, first:last]
        key_feat = feature(key_heads.astype(f32))
        delta_m = jnp.einsum("khd,khe->hde", key_feat, value_heads.astype(f32), precision=highest)
        delta_z = jnp.sum(key_feat, axis=0)
        delta = jnp.concatenate([delta_m, delta_z[:, None, :]], axis=1)
        pieces = []
        total = delta
        for k, step in enumerate(shifts):
            lo, hi = (cuts[k], cuts[k + 1])
            total, operands = lax.optimization_barrier(
                (total, (query_heads[:, lo:hi], key_heads[:, lo:hi], value_heads[:, lo:hi]))
            )
            perm = [(j, j + step) for j in range(n - step)]
            got = lax.ppermute(total, "ctx", perm)
            if hi > lo:
                piece = local_attention(*operands)
                got, piece = lax.optimization_barrier((got, piece))
                pieces.append(piece)
            total = total + jnp.where(me - step >= start, got, jnp.zeros_like(got))
        local_out = jnp.concatenate(pieces, axis=1)
        memory = total - delta
        mem_m = memory[:, :dh, :]
        mem_z = memory[:, dh, :]
        query_feat = feature(query_heads.astype(f32))
        numerator = jnp.einsum("qhd,hde->qhe", query_feat, mem_m, precision=highest)
        denominator = jnp.einsum("qhd,hd->qh", query_feat, mem_z, precision=highest)
        recalled = numerator / jnp.maximum(denominator, 1.0)[..., None]
        gate_value = gate_all[first:last][None, :, None]
        combined = (
            (gate_value * recalled + (1.0 - gate_value) * local_out)
            .astype(bf16)
            .reshape(seg, group_width)
        )
        outgoing = jnp.take(combined, pslot, axis=0, mode="clip").reshape(n, cap, group_width)
        incoming = lax.all_to_all(outgoing, "ctx", 0, 0, tiled=True).reshape(slots, group_width)
        rows = jnp.take(incoming, send_slot, axis=0, mode="clip")
        gathered = lax.all_gather(rows, "head", axis=1, tiled=True)
        part = jnp.dot(
            gathered,
            weight_rows[:, first:last].reshape(head_count * group_width, out_cols),
            preferred_element_type=f32,
        )
        return (part, combined)

    summed, hold = one_group(0, None)
    for g in range(1, len(bounds) - 1):
        part, hold = one_group(g, hold)
        summed = summed + part
    return summed.astype(bf16)


def solution(mesh):
    return jax.shard_map(
        per_device,
        mesh=mesh,
        in_specs=(
            P("ctx", "head"),
            P("ctx", "head"),
            P("ctx", "head"),
            P(),
            P(),
            P("head"),
            P(None, "head"),
        ),
        out_specs=P("ctx", "head"),
        check_vma=False,
    )
```

profile of v0, /device:TPU:1, one launch (start us, length us, event | category | flops | bytes accessed | tf_op | source)
XLA Modules:
  0.0 402.4 jit_solution(4213001769700298006)
XLA Ops:
  9.0 5.8 %gather_fusion.2 = bf16[1536,1024]{1,0:T(8,128)(2,1)} fusion(bf16[1024,1024]{1,0:T(8,128)(2,1)S(1)} %copy-done, s32[2048]{0:T(1024)S(1)} %pad_clamp_fusion.1), kind=kCustom, calls=%fused_computation.2 | custom fusion | bytes 6297600 | tf_op jit(solution)/shard_map/jit(_take)/gather | solution.py:59
  14.8 8.8 %all-to-all-start.1 = ((bf16[32,48,1024]{2,1,0:T(8,128)(2,1)}), bf16[32,48,1024]{2,1,0:T(8,128)(2,1)}, u32[]{:S(2)}, u32[]{:S(2)}) async-start(bf16[32,48,1024]{2,1,0:T(8,128)(2,1)} %bitcast.224), calls=%async_computation.1 | async-start | bytes 6291456 | tf_op jit(solution)/shard_map/all_to_all | solution.py:60
  23.6 5.8 %gather_fusion = bf16[1536,1024]{1,0:T(8,128)(2,1)} fusion(bf16[1024,1024]{1,0:T(8,128)(2,1)S(1)} %copy-done.2, s32[2048]{0:T(1024)S(1)} %pad_clamp_fusion.1), kind=kCustom, calls=%fused_computation | custom fusion | bytes 6297600 | tf_op jit(solution)/shard_map/jit(_take)/gather | solution.py:59
  29.5 34.0 %all-to-all-done.1 = bf16[32,48,1024]{2,1,0:T(8,128)(2,1)} async-done(((bf16[32,48,1024]{2,1,0:T(8,128)(2,1)}), bf16[32,48,1024]{2,1,0:T(8,128)(2,1)}, u32[]{:S(2)}, u32[]{:S(2)}) %all-to-all-start.1) | async-done | bytes 3145760 | tf_op jit(solution)/shard_map/all_to_all | solution.py:60
  71.9 5.8 %gather_fusion.4 = bf16[1536,1024]{1,0:T(8,128)(2,1)} fusion(bf16[1024,1024]{1,0:T(8,128)(2,1)S(1)} %copy-done.3, s32[2048]{0:T(1024)S(1)} %pad_clamp_fusion.1), kind=kCustom, calls=%fused_computation.4 | custom fusion | bytes 6297600 | tf_op jit(solution)/shard_map/jit(_take)/gather | solution.py:59
  79.1 29.2 %all-to-all-done = bf16[32,48,1024]{2,1,0:T(8,128)(2,1)} async-done(((bf16[32,48,1024]{2,1,0:T(8,128)(2,1)}), bf16[32,48,1024]{2,1,0:T(8,128)(2,1)}, u32[]{:S(2)}, u32[]{:S(2)}) %all-to-all-start) | async-done | bytes 3145760 | tf_op jit(solution)/shard_map/all_to_all | solution.py:60
  108.3 5.3 %all-to-all-start.2 = ((bf16[32,48,1024]{2,1,0:T(8,128)(2,1)}), bf16[32,48,1024]{2,1,0:T(8,128)(2,1)S(1)}, u32[]{:S(2)}, u32[]{:S(2)}) async-start(bf16[32,48,1024]{2,1,0:T(8,128)(2,1)} %bitcast.222), calls=%async_computation.2 | async-start | bytes 6291456 | tf_op jit(solution)/shard_map/all_to_all | solution.py:60
  118.1 8.3 %gather_fusion.3 = bf16[1024,1024]{1,0:T(8,128)(2,1)} fusion(bf16[1536,1024]{1,0:T(8,128)(2,1)} %bitcast.6, s32[1024]{0:T(1024)S(1)} %broadcast_clamp_fusion.1), kind=kCustom, calls=%fused_computation.3 | custom fusion | bytes 4198400 | tf_op jit(solution)/shard_map/jit(_take)/gather | solution.py:61
  130.4 8.3 %gather_fusion.1 = bf16[1024,1024]{1,0:T(8,128)(2,1)} fusion(bf16[1536,1024]{1,0:T(8,128)(2,1)} %bitcast.4, s32[1024]{0:T(1024)S(1)} %broadcast_clamp_fusion.1), kind=kCustom, calls=%fused_computation.1 | custom fusion | bytes 4198400 | tf_op jit(solution)/shard_map/jit(_take)/gather | solution.py:61
  155.9 5.3 %gather_fusion.5 = bf16[1024,1024]{1,0:T(8,128)(2,1)} fusion(bf16[1536,1024]{1,0:T(8,128)(2,1)S(1)} %bitcast.215, s32[1024]{0:T(1024)S(1)} %broadcast_clamp_fusion.1), kind=kCustom, calls=%fused_computation.5 | custom fusion | bytes 4198400 | tf_op jit(solution)/shard_map/jit(_take)/gather | solution.py:61
  200.6 6.2 %collective-permute-start.3 = (f32[4,129,128]{2,1,0:T(8,128)S(1)}, f32[4,129,128]{2,1,0:T(8,128)S(1)}, u32[]{:S(2)}, u32[]{:S(2)}) collective-permute-start(f32[4,129,128]{2,1,0:T(8,128)S(1)} %select_add_fusion.5), channel_id=1, source_target_pairs={{0,32},{4,36},{8,40},{12,44},{16,48},{20,52},{24,56},{28,60},{32,6... | collective-permute-start | bytes 792584 | tf_op jit(solution)/shard_map/ppermute | solution.py:99
  210.3 5.5 %collective-permute-start.4 = (f32[4,129,128]{2,1,0:T(8,128)S(1)}, f32[4,129,128]{2,1,0:T(8,128)S(1)}, u32[]{:S(2)}, u32[]{:S(2)}) collective-permute-start(f32[4,129,128]{2,1,0:T(8,128)S(1)} %select_add_fusion.4), channel_id=1, source_target_pairs={{0,64},{4,68},{8,72},{12,76},{16,80},{20,84},{24,88},{28,92},{32,9... | collective-permute-start | bytes 792584 | tf_op jit(solution)/shard_map/ppermute | solution.py:99
  227.5 5.4 %gather_fusion.6 = bf16[1536,512]{1,0:T(8,128)(2,1)} fusion(bf16[1024,512]{1,0:T(8,128)(2,1)S(1)} %copy.61, s32[2048]{0:T(1024)S(1)} %pad_clamp_fusion), kind=kCustom, calls=%fused_computation.6 | custom fusion | bytes 3151872 | tf_op jit(solution)/shard_map/jit(_take)/gather | solution.py:119
  232.9 11.0 %all-to-all-start.3 = ((bf16[32,48,512]{2,1,0:T(8,128)(2,1)}), bf16[32,48,512]{2,1,0:T(8,128)(2,1)S(1)}, u32[]{:S(2)}, u32[]{:S(2)}) async-start(bf16[32,48,512]{2,1,0:T(8,128)(2,1)} %bitcast.39), calls=%async_computation.3 | async-start | bytes 3145728 | tf_op jit(solution)/shard_map/all_to_all | solution.py:120
  249.0 6.0 %collective-permute-start.7 = (f32[4,129,128]{2,1,0:T(8,128)S(1)}, f32[4,129,128]{2,1,0:T(8,128)S(1)}, u32[]{:S(2)}, u32[]{:S(2)}) collective-permute-start(f32[4,129,128]{2,1,0:T(8,128)S(1)} %select_add_fusion.2), channel_id=1, source_target_pairs={{0,16},{4,20},{8,24},{12,28},{16,32},{20,36},{24,40},{28,44},{32,4... | collective-permute-start | bytes 792584 | tf_op jit(solution)/shard_map/ppermute | solution.py:99
  256.7 9.9 %all-to-all-done.3 = bf16[32,48,512]{2,1,0:T(8,128)(2,1)S(1)} async-done(((bf16[32,48,512]{2,1,0:T(8,128)(2,1)}), bf16[32,48,512]{2,1,0:T(8,128)(2,1)S(1)}, u32[]{:S(2)}, u32[]{:S(2)}) %all-to-all-start.3) | async-done | bytes 1572896 | tf_op jit(solution)/shard_map/all_to_all | solution.py:120
  266.6 5.1 %gather_fusion.7 = bf16[1024,512]{1,0:T(8,128)(2,1)} fusion(bf16[1536,512]{1,0:T(8,128)(2,1)S(1)} %bitcast.216, s32[1024]{0:T(1024)S(1)} %broadcast_clamp_fusion), kind=kCustom, calls=%fused_computation.7 | custom fusion | bytes 2101248 | tf_op jit(solution)/shard_map/jit(_take)/gather | solution.py:121
  278.8 6.7 %collective-permute-start.9 = (f32[4,129,128]{2,1,0:T(8,128)S(1)}, f32[4,129,128]{2,1,0:T(8,128)S(1)}, u32[]{:S(2)}, u32[]{:S(2)}) collective-permute-start(f32[4,129,128]{2,1,0:T(8,128)S(1)} %select_add_fusion), channel_id=1, source_target_pairs={{0,64},{4,68},{8,72},{12,76},{16,80},{20,84},{24,88},{28,92},{32,9... | collective-permute-start | bytes 792584 | tf_op jit(solution)/shard_map/ppermute | solution.py:99
  301.4 31.2 %all_to_all.25 = bf16[32,48,512]{2,1,0:T(8,128)(2,1)S(1)} all-to-all(bf16[32,48,512]{2,1,0:T(8,128)(2,1)S(1)} %bitcast.231), channel_id=1, replica_groups=mesh['ctx'=32,'head'=4] {'ctx'}, dimensions={0} | all-to-all | bytes 3145728 | tf_op jit(solution)/shard_map/all_to_all | solution.py:120
  332.6 5.0 %gather_fusion.9 = bf16[1024,512]{1,0:T(8,128)(2,1)} fusion(bf16[1536,512]{1,0:T(8,128)(2,1)S(1)} %bitcast.217, s32[1024]{0:T(1024)S(1)} %broadcast_clamp_fusion), kind=kCustom, calls=%fused_computation.9 | custom fusion | bytes 2101248 | tf_op jit(solution)/shard_map/jit(_take)/gather | solution.py:121
  337.7 6.1 %fusion.164 = (bf16[4,4,128,1024]{3,2,1,0:T(8,128)(2,1)}, bf16[4,4,128,1024]{3,2,1,0:T(8,128)(2,1)}) fusion(bf16[4,8,128,1024]{3,2,1,0:T(8,128)(2,1)} %bitcast.227), kind=kLoop, calls=%fused_computation.258 | loop fusion | bytes 16777216 | tf_op jit(solution)/shard_map/slice | solution.py:125
  343.8 10.6 %fusion.171 = f32[1024,1024]{1,0:T(8,128)} fusion(bf16[1024,2048]{1,0:T(8,128)(2,1)} %all-gather.5.cloned.1.call-done, bf16[2048,1024]{1,0:T(8,128)(2,1)} %bitcast.233), kind=kOutput, calls=%fused_computation.265 | convolution fusion | flops 4294967296 | bytes 12582912 | tf_op jit(solution)/shard_map/dot_general | solution.py:123
  354.4 30.2 %all-gather.7.cloned.1.call-done = bf16[1024,2048]{1,0:T(8,128)(2,1)} async-done(((bf16[1024,512]{1,0:T(8,128)(2,1)}), bf16[1024,2048]{1,0:T(8,128)(2,1)}) %all-gather.7.cloned.1.call-update) | async-done | bytes 4194320 | tf_op jit(solution)/shard_map/all_gather | solution.py:122
  384.5 10.6 %add_convert_fusion = bf16[1024,1024]{1,0:T(8,128)(2,1)} fusion(f32[1024,1024]{1,0:T(8,128)} %fusion.171, bf16[1024,2048]{1,0:T(8,128)(2,1)} %all-gather.7.cloned.1.call-done, bf16[2048,1024]{1,0:T(8,128)(2,1)} %bitcast.232), kind=kOutput, calls=%fused_computation.26 | convolution fusion | flops 4297064448 | bytes 14680064 | tf_op jit(solution)/shard_map/dot_general | solution.py:123
  (179 shorter events, 118.4 us)
Async XLA Ops:
  7.6 61.5 %copy-start.16 = (s32[32,1024]{1,0:T(8,128)}, s32[32,1024]{1,0:T(8,128)S(1)}, u32[]{:S(2)}) copy-start(s32[32,1024]{1,0:T(8,128)S(1)} %reshape.467) | copy-start | bytes 393220
  14.8 48.6 %all-to-all-start.1 = ((bf16[32,48,1024]{2,1,0:T(8,128)(2,1)}), bf16[32,48,1024]{2,1,0:T(8,128)(2,1)}, u32[]{:S(2)}, u32[]{:S(2)}) async-start(bf16[32,48,1024]{2,1,0:T(8,128)(2,1)} %bitcast.224), calls=%async_computation.1 | async-start | bytes 6291456 | tf_op jit(solution)/shard_map/all_to_all | solution.py:60
  29.5 39.0 %copy-start.27 = (s32[32]{0:T(128)S(1)}, s32[32]{0:T(128)}, u32[]{:S(2)}) copy-start(s32[32]{0:T(128)} %param.11) | copy-start | bytes 388
  29.5 42.4 %copy-start.3 = (bf16[1024,1024]{1,0:T(8,128)(2,1)S(1)}, bf16[1024,1024]{1,0:T(8,128)(2,1)}, u32[]{:S(2)}) copy-start(bf16[1024,1024]{1,0:T(8,128)(2,1)} %param.7) | copy-start | bytes 6291460
  63.4 44.9 %all-to-all-start = ((bf16[32,48,1024]{2,1,0:T(8,128)(2,1)}), bf16[32,48,1024]{2,1,0:T(8,128)(2,1)}, u32[]{:S(2)}, u32[]{:S(2)}) async-start(bf16[32,48,1024]{2,1,0:T(8,128)(2,1)} %bitcast.223), calls=%async_computation | async-start | bytes 6291456 | tf_op jit(solution)/shard_map/all_to_all | solution.py:60
  108.3 47.6 %all-to-all-start.2 = ((bf16[32,48,1024]{2,1,0:T(8,128)(2,1)}), bf16[32,48,1024]{2,1,0:T(8,128)(2,1)S(1)}, u32[]{:S(2)}, u32[]{:S(2)}) async-start(bf16[32,48,1024]{2,1,0:T(8,128)(2,1)} %bitcast.222), calls=%async_computation.2 | async-start | bytes 6291456 | tf_op jit(solution)/shard_map/all_to_all | solution.py:60
  167.3 13.4 %collective-permute-start = (f32[4,129,128]{2,1,0:T(8,128)S(1)}, f32[4,129,128]{2,1,0:T(8,128)S(1)}, u32[]{:S(2)}, u32[]{:S(2)}) collective-permute-start(f32[4,129,128]{2,1,0:T(8,128)S(1)} %pad_maximum_fusion), channel_id=1, source_target_pairs={{0,4},{4,8},{8,12},{12,16},{16,20},{20,24},{24,28},{28,32},{32,36}... | collective-permute-start | bytes 792584 | tf_op jit(solution)/shard_map/ppermute | solution.py:99
  171.0 12.9 %collective-permute-start.5 = (f32[4,129,128]{2,1,0:T(8,128)S(1)}, f32[4,129,128]{2,1,0:T(8,128)S(1)}, u32[]{:S(2)}, u32[]{:S(2)}) collective-permute-start(f32[4,129,128]{2,1,0:T(8,128)S(1)} %pad_maximum_fusion.1), channel_id=1, source_target_pairs={{0,4},{4,8},{8,12},{12,16},{16,20},{20,24},{24,28},{28,32},{32,36}... | collective-permute-start | bytes 792584 | tf_op jit(solution)/shard_map/ppermute | solution.py:99
  180.7 9.6 %collective-permute-start.1 = (f32[4,129,128]{2,1,0:T(8,128)S(1)}, f32[4,129,128]{2,1,0:T(8,128)S(1)}, u32[]{:S(2)}, u32[]{:S(2)}) collective-permute-start(f32[4,129,128]{2,1,0:T(8,128)S(1)} %select_add_fusion.7), channel_id=1, source_target_pairs={{0,8},{4,12},{8,16},{12,20},{16,24},{20,28},{24,32},{28,36},{32,40... | collective-permute-start | bytes 792584 | tf_op jit(solution)/shard_map/ppermute | solution.py:99
  183.9 65.1 %collective-permute-start.6 = (f32[4,129,128]{2,1,0:T(8,128)S(1)}, f32[4,129,128]{2,1,0:T(8,128)}, u32[]{:S(2)}, u32[]{:S(2)}) collective-permute-start(f32[4,129,128]{2,1,0:T(8,128)S(1)} %select_add_fusion.3), channel_id=1, source_target_pairs={{0,8},{4,12},{8,16},{12,20},{16,24},{20,28},{24,32},{28,36},{32,40... | collective-permute-start | bytes 792584 | tf_op jit(solution)/shard_map/ppermute | solution.py:99
  190.3 10.3 %collective-permute-start.2 = (f32[4,129,128]{2,1,0:T(8,128)S(1)}, f32[4,129,128]{2,1,0:T(8,128)S(1)}, u32[]{:S(2)}, u32[]{:S(2)}) collective-permute-start(f32[4,129,128]{2,1,0:T(8,128)S(1)} %select_add_fusion.6), channel_id=1, source_target_pairs={{0,16},{4,20},{8,24},{12,28},{16,32},{20,36},{24,40},{28,44},{32,4... | collective-permute-start | bytes 792584 | tf_op jit(solution)/shard_map/ppermute | solution.py:99
  200.6 9.6 %collective-permute-start.3 = (f32[4,129,128]{2,1,0:T(8,128)S(1)}, f32[4,129,128]{2,1,0:T(8,128)S(1)}, u32[]{:S(2)}, u32[]{:S(2)}) collective-permute-start(f32[4,129,128]{2,1,0:T(8,128)S(1)} %select_add_fusion.5), channel_id=1, source_target_pairs={{0,32},{4,36},{8,40},{12,44},{16,48},{20,52},{24,56},{28,60},{32,6... | collective-permute-start | bytes 792584 | tf_op jit(solution)/shard_map/ppermute | solution.py:99
  210.3 8.9 %collective-permute-start.4 = (f32[4,129,128]{2,1,0:T(8,128)S(1)}, f32[4,129,128]{2,1,0:T(8,128)S(1)}, u32[]{:S(2)}, u32[]{:S(2)}) collective-permute-start(f32[4,129,128]{2,1,0:T(8,128)S(1)} %select_add_fusion.4), channel_id=1, source_target_pairs={{0,64},{4,68},{8,72},{12,76},{16,80},{20,84},{24,88},{28,92},{32,9... | collective-permute-start | bytes 792584 | tf_op jit(solution)/shard_map/ppermute | solution.py:99
  232.9 14.0 %copy-start.19 = (bf16[1024,1,128]{0,2,1:T(8,128)(2,1)S(1)}, bf16[1024,1,128]{0,2,1:T(8,128)(2,1)}, u32[]{:S(2)}) copy-start(bf16[1024,1,128]{0,2,1:T(8,128)(2,1)} %get-tuple-element.86) | copy-start | bytes 786436
  232.9 33.7 %all-to-all-start.3 = ((bf16[32,48,512]{2,1,0:T(8,128)(2,1)}), bf16[32,48,512]{2,1,0:T(8,128)(2,1)S(1)}, u32[]{:S(2)}, u32[]{:S(2)}) async-start(bf16[32,48,512]{2,1,0:T(8,128)(2,1)} %bitcast.39), calls=%async_computation.3 | async-start | bytes 3145728 | tf_op jit(solution)/shard_map/all_to_all | solution.py:120
  243.9 99.8 %all-gather.5.cloned.1.call-start = ((), (), s32[]{:S(2)}) async-start(), calls=%async_computation.5 | async-start | bytes 5242880 | tf_op jit(solution)/shard_map/all_gather | solution.py:122
  247.4 9.2 %copy-start.7 = (bf16[1024,1,128]{2,1,0:T(2,128)(2,1)S(1)}, bf16[1024,1,128]{2,1,0:T(2,128)(2,1)}, u32[]{:S(2)}) copy-start(bf16[1024,1,128]{2,1,0:T(2,128)(2,1)} %get-tuple-element.119) | copy-start | bytes 786436
  247.4 9.2 %copy-start.6 = (bf16[1024,1,128]{2,1,0:T(2,128)(2,1)S(1)}, bf16[1024,1,128]{2,1,0:T(2,128)(2,1)}, u32[]{:S(2)}) copy-start(bf16[1024,1,128]{2,1,0:T(2,128)(2,1)} %get-tuple-element.120) | copy-start | bytes 786436
  249.0 22.7 %collective-permute-start.7 = (f32[4,129,128]{2,1,0:T(8,128)S(1)}, f32[4,129,128]{2,1,0:T(8,128)S(1)}, u32[]{:S(2)}, u32[]{:S(2)}) collective-permute-start(f32[4,129,128]{2,1,0:T(8,128)S(1)} %select_add_fusion.2), channel_id=1, source_target_pairs={{0,16},{4,20},{8,24},{12,28},{16,32},{20,36},{24,40},{28,44},{32,4... | collective-permute-start | bytes 792584 | tf_op jit(solution)/shard_map/ppermute | solution.py:99
  271.7 112.8 %all-gather.7.cloned.1.call-start = ((), (), s32[]{:S(2)}) async-start(), calls=%async_computation.6 | async-start | bytes 5242880 | tf_op jit(solution)/shard_map/all_gather | solution.py:122
  271.8 7.0 %collective-permute-start.8 = (f32[4,129,128]{2,1,0:T(8,128)S(1)}, f32[4,129,128]{2,1,0:T(8,128)S(1)}, u32[]{:S(2)}, u32[]{:S(2)}) collective-permute-start(f32[4,129,128]{2,1,0:T(8,128)S(1)} %select_add_fusion.1), channel_id=1, source_target_pairs={{0,32},{4,36},{8,40},{12,44},{16,48},{20,52},{24,56},{28,60},{32,6... | collective-permute-start | bytes 792584 | tf_op jit(solution)/shard_map/ppermute | solution.py:99
  275.1 10.5 %copy-start.25 = (bf16[1024,1,128]{2,0,1:T(8,128)(2,1)S(1)}, bf16[1024,1,128]{2,0,1:T(8,128)(2,1)}, u32[]{:S(2)}) copy-start(bf16[1024,1,128]{2,0,1:T(8,128)(2,1)} %copy.103) | copy-start | bytes 786436
  278.8 11.4 %collective-permute-start.9 = (f32[4,129,128]{2,1,0:T(8,128)S(1)}, f32[4,129,128]{2,1,0:T(8,128)S(1)}, u32[]{:S(2)}, u32[]{:S(2)}) collective-permute-start(f32[4,129,128]{2,1,0:T(8,128)S(1)} %select_add_fusion), channel_id=1, source_target_pairs={{0,64},{4,68},{8,72},{12,76},{16,80},{20,84},{24,88},{28,92},{32,9... | collective-permute-start | bytes 792584 | tf_op jit(solution)/shard_map/ppermute | solution.py:99
  384.5 10.6 %copy-start.1 = (bf16[1024,1024]{1,0:T(8,128)(2,1)S(1)}, bf16[1024,1024]{1,0:T(8,128)(2,1)}, u32[]{:S(2)}) copy-start(bf16[1024,1024]{1,0:T(8,128)(2,1)} %param.9) | copy-start | bytes 6291460
  (22 other events, 92.6 us)
Sparse Core Ops, SparseCore 0:
  271.8 51.0 all-gather.4
  337.8 46.6 all-gather.6
where the time goes:
time: 410 us; the launch traced here: 402 us
  waiting for transfers between devices  112 us (27%)
  local copies, waits for them, and re-layouts  92.6 us (23%)
  starting transfers between devices  73.5 us (18%)
  matrix products  60.1 us (15%)
  blocking collectives  31.2 us (8%)
  between operations  17.9 us (4%)
  other arithmetic  15.3 us (4%)
    all_to_all x3, waiting for transfers between devices, dispatch(): got = lax.all_to_all(buffer, 'ctx', 0, 0, tiled=True).reshape(slots, width)  63.2 us
    ppermute x10, starting transfers between devices, one_group(): got = lax.ppermute(total, 'ctx', perm)  43.3 us
    all_to_all x1, blocking collectives, one_group(): lax.all_to_all(outgoing, 'ctx', 0, 0, tiled=True)  31.2 us
    all_gather x2, waiting for transfers between devices, one_group(): gathered = lax.all_gather(rows, 'head', axis=1, tiled=True)  30.2 us
    gather x4, local copies, waits for them, and re-layouts, dispatch(): return jnp.take(got, tok_slot, axis=0, mode='clip').reshape(seg, heads, dh)  25.9 us
    dot_general x2, matrix products, one_group(): jnp.dot(gathered, weight_rows[:, first:last].reshape(head_count * group_w...  21.2 us
    all_to_all x3, starting transfers between devices, dispatch(): got = lax.all_to_all(buffer, 'ctx', 0, 0, tiled=True).reshape(slots, width)  19.1 us
    gather x3, local copies, waits for them, and re-layouts, dispatch(): jnp.take(source, slot_row, axis=0, mode='clip').reshape(n, cap, width)  17.5 us
  transfers between devices with their start and end apart: 16, of which 9 were waited for; matrix products, arithmetic and copies ran while one was open for 34% of the time, Pallas kernels for 0%

commit v1 on v0

--- a/solution.py
+++ b/solution.py
@@ -119,7 +119,10 @@
         outgoing = jnp.take(combined, pslot, axis=0, mode="clip").reshape(n, cap, group_width)
         incoming = lax.all_to_all(outgoing, "ctx", 0, 0, tiled=True).reshape(slots, group_width)
         rows = jnp.take(incoming, send_slot, axis=0, mode="clip")
-        gathered = lax.all_gather(rows, "head", axis=1, tiled=True)
+        wide_n = lax.axis_size("head")
+        runs = [wide_n if ix == 1 else 1 for ix in range(rows.ndim)]
+        near = jnp.tile(rows, runs)
+        gathered = lax.all_to_all(near, "head", split_axis=1, concat_axis=1, tiled=True)
         part = jnp.dot(
             gathered,
             weight_rows[:, first:last].reshape(head_count * group_width, out_cols),

time: 410 us -> 431 us (1.051)
  the two profiles are of different devices: /device:TPU:1 before, /device:TPU:0 now
where the time goes in v1:
time: 431 us; the launch traced here: 423 us
  waiting for transfers between devices  159 us (37%)
  local copies, waits for them, and re-layouts  109 us (25%)
  starting transfers between devices  77.8 us (18%)
  matrix products  59.7 us (14%)
  other arithmetic  13.2 us (3%)
  between operations  4.45 us (1%)
    all_to_all x2, waiting for transfers between devices, one_group(): lax.all_to_all(near, 'head', split_axis=1, concat_axis=1, tiled=True)  69.8 us
    all_to_all x3, waiting for transfers between devices, dispatch(): got = lax.all_to_all(buffer, 'ctx', 0, 0, tiled=True).reshape(slots, width)  62.9 us
    ppermute x10, starting transfers between devices, one_group(): got = lax.ppermute(total, 'ctx', perm)  40.1 us
    gather x4, local copies, waits for them, and re-layouts, dispatch(): return jnp.take(got, tok_slot, axis=0, mode='clip').reshape(seg, heads, dh)  25.9 us
    all_to_all x2, waiting for transfers between devices, one_group(): lax.all_to_all(outgoing, 'ctx', 0, 0, tiled=True)  25.3 us
    dot_general x2, matrix products, one_group(): jnp.dot(gathered, weight_rows[:, first:last].reshape(head_count * group_w...  20.7 us
    all_to_all x3, starting transfers between devices, dispatch(): got = lax.all_to_all(buffer, 'ctx', 0, 0, tiled=True).reshape(slots, width)  17.8 us
    gather x3, local copies, waits for them, and re-layouts, dispatch(): jnp.take(source, slot_row, axis=0, mode='clip').reshape(n, cap, width)  17.4 us
  transfers between devices with their start and end apart: 17, of which 8 were waited for; matrix products, arithmetic and copies ran while one was open for 33% of the time, Pallas kernels for 0%

profile of v1, /device:TPU:0, one launch (start us, length us, event | category | flops | bytes accessed | tf_op | source)
XLA Modules:
  0.0 422.7 jit_solution(5922814777215444623)
XLA Ops:
  2.5 5.8 %gather_fusion.2 = bf16[1536,1024]{1,0:T(8,128)(2,1)} fusion(bf16[1024,1024]{1,0:T(8,128)(2,1)S(1)} %copy-done, s32[2048]{0:T(1024)S(1)} %pad_clamp_fusion.1), kind=kCustom, calls=%fused_computation.2 | custom fusion | bytes 6297600 | tf_op jit(solution)/shard_map/jit(_take)/gather | solution.py:59
  8.3 7.7 %all-to-all-start.1 = ((bf16[32,48,1024]{2,1,0:T(8,128)(2,1)}), bf16[32,48,1024]{2,1,0:T(8,128)(2,1)}, u32[]{:S(2)}, u32[]{:S(2)}) async-start(bf16[32,48,1024]{2,1,0:T(8,128)(2,1)} %bitcast.225), calls=%async_computation.1 | async-start | bytes 6291456 | tf_op jit(solution)/shard_map/all_to_all | solution.py:60
  16.0 5.8 %gather_fusion = bf16[1536,1024]{1,0:T(8,128)(2,1)} fusion(bf16[1024,1024]{1,0:T(8,128)(2,1)S(1)} %copy-done.2, s32[2048]{0:T(1024)S(1)} %pad_clamp_fusion.1), kind=kCustom, calls=%fused_computation | custom fusion | bytes 6297600 | tf_op jit(solution)/shard_map/jit(_take)/gather | solution.py:59
  21.8 34.1 %all-to-all-done.1 = bf16[32,48,1024]{2,1,0:T(8,128)(2,1)} async-done(((bf16[32,48,1024]{2,1,0:T(8,128)(2,1)}), bf16[32,48,1024]{2,1,0:T(8,128)(2,1)}, u32[]{:S(2)}, u32[]{:S(2)}) %all-to-all-start.1) | async-done | bytes 3145760 | tf_op jit(solution)/shard_map/all_to_all | solution.py:60
  64.2 5.8 %gather_fusion.4 = bf16[1536,1024]{1,0:T(8,128)(2,1)} fusion(bf16[1024,1024]{1,0:T(8,128)(2,1)S(1)} %copy-done.3, s32[2048]{0:T(1024)S(1)} %pad_clamp_fusion.1), kind=kCustom, calls=%fused_computation.4 | custom fusion | bytes 6297600 | tf_op jit(solution)/shard_map/jit(_take)/gather | solution.py:59
  72.0 28.8 %all-to-all-done = bf16[32,48,1024]{2,1,0:T(8,128)(2,1)} async-done(((bf16[32,48,1024]{2,1,0:T(8,128)(2,1)}), bf16[32,48,1024]{2,1,0:T(8,128)(2,1)}, u32[]{:S(2)}, u32[]{:S(2)}) %all-to-all-start) | async-done | bytes 3145760 | tf_op jit(solution)/shard_map/all_to_all | solution.py:60
  110.5 8.3 %gather_fusion.3 = bf16[1024,1024]{1,0:T(8,128)(2,1)} fusion(bf16[1536,1024]{1,0:T(8,128)(2,1)} %bitcast.6, s32[1024]{0:T(1024)S(1)} %broadcast_clamp_fusion.1), kind=kCustom, calls=%fused_computation.3 | custom fusion | bytes 4198400 | tf_op jit(solution)/shard_map/jit(_take)/gather | solution.py:61
  122.7 8.3 %gather_fusion.1 = bf16[1024,1024]{1,0:T(8,128)(2,1)} fusion(bf16[1536,1024]{1,0:T(8,128)(2,1)} %bitcast.4, s32[1024]{0:T(1024)S(1)} %broadcast_clamp_fusion.1), kind=kCustom, calls=%fused_computation.1 | custom fusion | bytes 4198400 | tf_op jit(solution)/shard_map/jit(_take)/gather | solution.py:61
  148.5 5.3 %gather_fusion.5 = bf16[1024,1024]{1,0:T(8,128)(2,1)} fusion(bf16[1536,1024]{1,0:T(8,128)(2,1)S(1)} %bitcast.217, s32[1024]{0:T(1024)S(1)} %broadcast_clamp_fusion.1), kind=kCustom, calls=%fused_computation.5 | custom fusion | bytes 4198400 | tf_op jit(solution)/shard_map/jit(_take)/gather | solution.py:61
  201.2 6.2 %collective-permute-start.8 = (f32[4,129,128]{2,1,0:T(8,128)S(1)}, f32[4,129,128]{2,1,0:T(8,128)S(1)}, u32[]{:S(2)}, u32[]{:S(2)}) collective-permute-start(f32[4,129,128]{2,1,0:T(8,128)S(1)} %select_add_fusion.1), channel_id=1, source_target_pairs={{0,32},{4,36},{8,40},{12,44},{16,48},{20,52},{24,56},{28,60},{32,6... | collective-permute-start | bytes 792584 | tf_op jit(solution)/shard_map/ppermute | solution.py:99
  213.0 5.7 %collective-permute-start.4 = (f32[4,129,128]{2,1,0:T(8,128)S(1)}, f32[4,129,128]{2,1,0:T(8,128)S(1)}, u32[]{:S(2)}, u32[]{:S(2)}) collective-permute-start(f32[4,129,128]{2,1,0:T(8,128)S(1)} %select_add_fusion.4), channel_id=1, source_target_pairs={{0,64},{4,68},{8,72},{12,76},{16,80},{20,84},{24,88},{28,92},{32,9... | collective-permute-start | bytes 792584 | tf_op jit(solution)/shard_map/ppermute | solution.py:99
  231.6 5.4 %gather_fusion.6 = bf16[1536,512]{1,0:T(8,128)(2,1)} fusion(bf16[1024,512]{1,0:T(8,128)(2,1)S(1)} %copy.121, s32[2048]{0:T(1024)S(1)} %pad_clamp_fusion), kind=kCustom, calls=%fused_computation.6 | custom fusion | bytes 3151872 | tf_op jit(solution)/shard_map/jit(_take)/gather | solution.py:119
  253.3 5.4 %gather_fusion.8 = bf16[1536,512]{1,0:T(8,128)(2,1)} fusion(bf16[1024,512]{1,0:T(8,128)(2,1)S(1)} %copy.136, s32[2048]{0:T(1024)S(1)} %pad_clamp_fusion), kind=kCustom, calls=%fused_computation.8 | custom fusion | bytes 3151872 | tf_op jit(solution)/shard_map/jit(_take)/gather | solution.py:119
  258.7 6.3 %all-to-all-done.3 = bf16[32,48,512]{2,1,0:T(8,128)(2,1)S(1)} async-done(((bf16[32,48,512]{2,1,0:T(8,128)(2,1)}), bf16[32,48,512]{2,1,0:T(8,128)(2,1)S(1)}, u32[]{:S(2)}, u32[]{:S(2)}) %all-to-all-start.3) | async-done | bytes 1572896 | tf_op jit(solution)/shard_map/all_to_all | solution.py:120
  273.7 19.1 %all-to-all-done.5 = bf16[32,48,512]{2,1,0:T(8,128)(2,1)} async-done(((bf16[32,48,512]{2,1,0:T(8,128)(2,1)}), bf16[32,48,512]{2,1,0:T(8,128)(2,1)}, u32[]{:S(2)}, u32[]{:S(2)}) %all-to-all-start.5) | async-done | bytes 1572896 | tf_op jit(solution)/shard_map/all_to_all | solution.py:120
  295.1 5.3 %all-to-all-start.4 = ((bf16[1024,4,512]{2,0,1:T(8,128)(2,1)}), bf16[1024,4,512]{2,0,1:T(8,128)(2,1)}, u32[]{:S(2)}, u32[]{:S(2)}) async-start(bf16[1024,4,512]{2,0,1:T(8,128)(2,1)} %tile.4), calls=%async_computation.4 | async-start | bytes 8388608 | tf_op jit(solution)/shard_map/all_to_all | solution.py:125
  300.4 5.6 %gather_fusion.9 = bf16[1024,512]{1,0:T(8,128)(2,1)S(1)} fusion(bf16[1536,512]{1,0:T(8,128)(2,1)} %bitcast.76, s32[1024]{0:T(1024)S(1)} %broadcast_clamp_fusion), kind=kCustom, calls=%fused_computation.9 | custom fusion | bytes 2101248 | tf_op jit(solution)/shard_map/jit(_take)/gather | solution.py:121
  306.0 43.9 %all-to-all-done.4 = bf16[1024,4,512]{2,0,1:T(8,128)(2,1)} async-done(((bf16[1024,4,512]{2,0,1:T(8,128)(2,1)}), bf16[1024,4,512]{2,0,1:T(8,128)(2,1)}, u32[]{:S(2)}, u32[]{:S(2)}) %all-to-all-start.4) | async-done | bytes 4194336 | tf_op jit(solution)/shard_map/all_to_all | solution.py:125
  357.2 6.1 %fusion.164 = (bf16[4,4,128,1024]{3,2,1,0:T(8,128)(2,1)}, bf16[4,4,128,1024]{3,2,1,0:T(8,128)(2,1)}) fusion(bf16[4,8,128,1024]{3,2,1,0:T(8,128)(2,1)} %bitcast.228), kind=kLoop, calls=%fused_computation.258 | loop fusion | bytes 16777216 | tf_op jit(solution)/shard_map/slice | solution.py:128
  363.2 6.4 %copy.122 = bf16[1024,4,512]{0,2,1:T(8,128)(2,1)} copy(bf16[1024,4,512]{2,0,1:T(8,128)(2,1)} %all-to-all-done.4) | data formatting | bytes 8388608 | tf_op jit(solution)/shard_map/all_to_all | solution.py:125
  369.6 10.0 %fusion.171 = f32[1024,1024]{1,0:T(8,128)} fusion(bf16[1024,2048]{0,1:T(8,128)(2,1)} %bitcast.235, bf16[2048,1024]{1,0:T(8,128)(2,1)} %bitcast.237), kind=kOutput, calls=%fused_computation.265 | convolution fusion | flops 4294967296 | bytes 12582912 | tf_op jit(solution)/shard_map/dot_general | solution.py:126
  379.6 25.9 %all-to-all-done.6 = bf16[1024,4,512]{2,0,1:T(8,128)(2,1)} async-done(((bf16[1024,4,512]{2,0,1:T(8,128)(2,1)}), bf16[1024,4,512]{2,0,1:T(8,128)(2,1)}, u32[]{:S(2)}, u32[]{:S(2)}) %all-to-all-start.6) | async-done | bytes 4194336 | tf_op jit(solution)/shard_map/all_to_all | solution.py:125
  405.5 6.3 %copy.137 = bf16[1024,4,512]{0,2,1:T(8,128)(2,1)} copy(bf16[1024,4,512]{2,0,1:T(8,128)(2,1)} %all-to-all-done.6) | data formatting | bytes 8388608 | tf_op jit(solution)/shard_map/all_to_all | solution.py:125
  411.8 10.7 %add_convert_fusion = bf16[1024,1024]{1,0:T(8,128)(2,1)} fusion(f32[1024,1024]{1,0:T(8,128)} %fusion.171, bf16[1024,2048]{0,1:T(8,128)(2,1)} %bitcast.234, bf16[2048,1024]{1,0:T(8,128)(2,1)} %bitcast.236), kind=kOutput, calls=%fused_computation.26 | convolution fusion | flops 4297064448 | bytes 14680064 | tf_op jit(solution)/shard_map/dot_general | solution.py:126
  (192 shorter events, 140.2 us)
Async XLA Ops:
  8.3 7.7 %copy-start.2 = (bf16[1024,1024]{1,0:T(8,128)(2,1)S(1)}, bf16[1024,1024]{1,0:T(8,128)(2,1)}, u32[]{:S(2)}) copy-start(bf16[1024,1024]{1,0:T(8,128)(2,1)} %param.8) | copy-start | bytes 6291460
  8.3 47.6 %all-to-all-start.1 = ((bf16[32,48,1024]{2,1,0:T(8,128)(2,1)}), bf16[32,48,1024]{2,1,0:T(8,128)(2,1)}, u32[]{:S(2)}, u32[]{:S(2)}) async-start(bf16[32,48,1024]{2,1,0:T(8,128)(2,1)} %bitcast.225), calls=%async_computation.1 | async-start | bytes 6291456 | tf_op jit(solution)/shard_map/all_to_all | solution.py:60
  21.7 39.1 %copy-start.31 = (s32[32]{0:T(128)S(1)}, s32[32]{0:T(128)}, u32[]{:S(2)}) copy-start(s32[32]{0:T(128)} %param.11) | copy-start | bytes 388
  21.7 42.4 %copy-start.3 = (bf16[1024,1024]{1,0:T(8,128)(2,1)S(1)}, bf16[1024,1024]{1,0:T(8,128)(2,1)}, u32[]{:S(2)}) copy-start(bf16[1024,1024]{1,0:T(8,128)(2,1)} %param.7) | copy-start | bytes 6291460
  55.9 44.9 %all-to-all-start = ((bf16[32,48,1024]{2,1,0:T(8,128)(2,1)}), bf16[32,48,1024]{2,1,0:T(8,128)(2,1)}, u32[]{:S(2)}, u32[]{:S(2)}) async-start(bf16[32,48,1024]{2,1,0:T(8,128)(2,1)} %bitcast.224), calls=%async_computation | async-start | bytes 6291456 | tf_op jit(solution)/shard_map/all_to_all | solution.py:60
  100.8 47.8 %all-to-all-start.2 = ((bf16[32,48,1024]{2,1,0:T(8,128)(2,1)}), bf16[32,48,1024]{2,1,0:T(8,128)(2,1)S(1)}, u32[]{:S(2)}, u32[]{:S(2)}) async-start(bf16[32,48,1024]{2,1,0:T(8,128)(2,1)} %bitcast.223), calls=%async_computation.2 | async-start | bytes 6291456 | tf_op jit(solution)/shard_map/all_to_all | solution.py:60
  160.2 11.8 %collective-permute-start = (f32[4,129,128]{2,1,0:T(8,128)S(1)}, f32[4,129,128]{2,1,0:T(8,128)S(1)}, u32[]{:S(2)}, u32[]{:S(2)}) collective-permute-start(f32[4,129,128]{2,1,0:T(8,128)S(1)} %pad_maximum_fusion), channel_id=1, source_target_pairs={{0,4},{4,8},{8,12},{12,16},{16,20},{20,24},{24,28},{28,32},{32,36}... | collective-permute-start | bytes 792584 | tf_op jit(solution)/shard_map/ppermute | solution.py:99
  162.7 12.8 %collective-permute-start.5 = (f32[4,129,128]{2,1,0:T(8,128)S(1)}, f32[4,129,128]{2,1,0:T(8,128)S(1)}, u32[]{:S(2)}, u32[]{:S(2)}) collective-permute-start(f32[4,129,128]{2,1,0:T(8,128)S(1)} %pad_maximum_fusion.1), channel_id=1, source_target_pairs={{0,4},{4,8},{8,12},{12,16},{16,20},{20,24},{24,28},{28,32},{32,36}... | collective-permute-start | bytes 792584 | tf_op jit(solution)/shard_map/ppermute | solution.py:99
  172.1 12.4 %collective-permute-start.1 = (f32[4,129,128]{2,1,0:T(8,128)S(1)}, f32[4,129,128]{2,1,0:T(8,128)S(1)}, u32[]{:S(2)}, u32[]{:S(2)}) collective-permute-start(f32[4,129,128]{2,1,0:T(8,128)S(1)} %select_add_fusion.7), channel_id=1, source_target_pairs={{0,8},{4,12},{8,16},{12,20},{16,24},{20,28},{24,32},{28,36},{32,40... | collective-permute-start | bytes 792584 | tf_op jit(solution)/shard_map/ppermute | solution.py:99
  175.5 14.0 %collective-permute-start.6 = (f32[4,129,128]{2,1,0:T(8,128)S(1)}, f32[4,129,128]{2,1,0:T(8,128)S(1)}, u32[]{:S(2)}, u32[]{:S(2)}) collective-permute-start(f32[4,129,128]{2,1,0:T(8,128)S(1)} %select_add_fusion.3), channel_id=1, source_target_pairs={{0,8},{4,12},{8,16},{12,20},{16,24},{20,28},{24,32},{28,36},{32,40... | collective-permute-start | bytes 792584 | tf_op jit(solution)/shard_map/ppermute | solution.py:99
  184.5 11.5 %copy-start.9 = (bf16[1024,1,128]{2,1,0:T(2,128)(2,1)S(1)}, bf16[1024,1,128]{2,1,0:T(2,128)(2,1)}, u32[]{:S(2)}) copy-start(bf16[1024,1,128]{2,1,0:T(2,128)(2,1)} %get-tuple-element.119) | copy-start | bytes 786436
  184.5 12.1 %collective-permute-start.2 = (f32[4,129,128]{2,1,0:T(8,128)S(1)}, f32[4,129,128]{2,1,0:T(8,128)S(1)}, u32[]{:S(2)}, u32[]{:S(2)}) collective-permute-start(f32[4,129,128]{2,1,0:T(8,128)S(1)} %select_add_fusion.6), channel_id=1, source_target_pairs={{0,16},{4,20},{8,24},{12,28},{16,32},{20,36},{24,40},{28,44},{32,4... | collective-permute-start | bytes 792584 | tf_op jit(solution)/shard_map/ppermute | solution.py:99
  189.6 11.5 %collective-permute-start.7 = (f32[4,129,128]{2,1,0:T(8,128)S(1)}, f32[4,129,128]{2,1,0:T(8,128)S(1)}, u32[]{:S(2)}, u32[]{:S(2)}) collective-permute-start(f32[4,129,128]{2,1,0:T(8,128)S(1)} %select_add_fusion.2), channel_id=1, source_target_pairs={{0,16},{4,20},{8,24},{12,28},{16,32},{20,36},{24,40},{28,44},{32,4... | collective-permute-start | bytes 792584 | tf_op jit(solution)/shard_map/ppermute | solution.py:99
  196.6 16.3 %collective-permute-start.3 = (f32[4,129,128]{2,1,0:T(8,128)S(1)}, f32[4,129,128]{2,1,0:T(8,128)S(1)}, u32[]{:S(2)}, u32[]{:S(2)}) collective-permute-start(f32[4,129,128]{2,1,0:T(8,128)S(1)} %select_add_fusion.5), channel_id=1, source_target_pairs={{0,32},{4,36},{8,40},{12,44},{16,48},{20,52},{24,56},{28,60},{32,6... | collective-permute-start | bytes 792584 | tf_op jit(solution)/shard_map/ppermute | solution.py:99
  201.2 7.4 %copy-start.18 = (bf16[1024,1,128]{0,2,1:T(8,128)(2,1)S(1)}, bf16[1024,1,128]{0,2,1:T(8,128)(2,1)}, u32[]{:S(2)}) copy-start(bf16[1024,1,128]{0,2,1:T(8,128)(2,1)} %get-tuple-element.67) | copy-start | bytes 786436
  201.2 17.5 %collective-permute-start.8 = (f32[4,129,128]{2,1,0:T(8,128)S(1)}, f32[4,129,128]{2,1,0:T(8,128)S(1)}, u32[]{:S(2)}, u32[]{:S(2)}) collective-permute-start(f32[4,129,128]{2,1,0:T(8,128)S(1)} %select_add_fusion.1), channel_id=1, source_target_pairs={{0,32},{4,36},{8,40},{12,44},{16,48},{20,52},{24,56},{28,60},{32,6... | collective-permute-start | bytes 792584 | tf_op jit(solution)/shard_map/ppermute | solution.py:99
  213.0 12.4 %collective-permute-start.4 = (f32[4,129,128]{2,1,0:T(8,128)S(1)}, f32[4,129,128]{2,1,0:T(8,128)S(1)}, u32[]{:S(2)}, u32[]{:S(2)}) collective-permute-start(f32[4,129,128]{2,1,0:T(8,128)S(1)} %select_add_fusion.4), channel_id=1, source_target_pairs={{0,64},{4,68},{8,72},{12,76},{16,80},{20,84},{24,88},{28,92},{32,9... | collective-permute-start | bytes 792584 | tf_op jit(solution)/shard_map/ppermute | solution.py:99
  218.8 26.2 %collective-permute-start.9 = (f32[4,129,128]{2,1,0:T(8,128)S(1)}, f32[4,129,128]{2,1,0:T(8,128)}, u32[]{:S(2)}, u32[]{:S(2)}) collective-permute-start(f32[4,129,128]{2,1,0:T(8,128)S(1)} %select_add_fusion), channel_id=1, source_target_pairs={{0,64},{4,68},{8,72},{12,76},{16,80},{20,84},{24,88},{28,92},{32,9... | collective-permute-start | bytes 792584 | tf_op jit(solution)/shard_map/ppermute | solution.py:99
  237.0 28.0 %all-to-all-start.3 = ((bf16[32,48,512]{2,1,0:T(8,128)(2,1)}), bf16[32,48,512]{2,1,0:T(8,128)(2,1)S(1)}, u32[]{:S(2)}, u32[]{:S(2)}) async-start(bf16[32,48,512]{2,1,0:T(8,128)(2,1)} %bitcast.232), calls=%async_computation.3 | async-start | bytes 3145728 | tf_op jit(solution)/shard_map/all_to_all | solution.py:120
  253.3 16.4 %copy-start.24 = (s32[1024]{0:T(1024)S(1)}, s32[1024]{0:T(1024)}, u32[]{:S(2)}) copy-start(s32[1024]{0:T(1024)} %copy-done.23) | copy-start | bytes 12292
  265.0 27.8 %all-to-all-start.5 = ((bf16[32,48,512]{2,1,0:T(8,128)(2,1)}), bf16[32,48,512]{2,1,0:T(8,128)(2,1)}, u32[]{:S(2)}, u32[]{:S(2)}) async-start(bf16[32,48,512]{2,1,0:T(8,128)(2,1)} %bitcast.233), calls=%async_computation.5 | async-start | bytes 3145728 | tf_op jit(solution)/shard_map/all_to_all | solution.py:120
  295.1 54.8 %all-to-all-start.4 = ((bf16[1024,4,512]{2,0,1:T(8,128)(2,1)}), bf16[1024,4,512]{2,0,1:T(8,128)(2,1)}, u32[]{:S(2)}, u32[]{:S(2)}) async-start(bf16[1024,4,512]{2,0,1:T(8,128)(2,1)} %tile.4), calls=%async_computation.4 | async-start | bytes 8388608 | tf_op jit(solution)/shard_map/all_to_all | solution.py:125
  352.1 53.3 %all-to-all-start.6 = ((bf16[1024,4,512]{2,0,1:T(8,128)(2,1)}), bf16[1024,4,512]{2,0,1:T(8,128)(2,1)}, u32[]{:S(2)}, u32[]{:S(2)}) async-start(bf16[1024,4,512]{2,0,1:T(8,128)(2,1)} %tile.5), calls=%async_computation.6 | async-start | bytes 8388608 | tf_op jit(solution)/shard_map/all_to_all | solution.py:125
  411.8 10.7 %copy-start.1 = (bf16[1024,1024]{1,0:T(8,128)(2,1)S(1)}, bf16[1024,1024]{1,0:T(8,128)(2,1)}, u32[]{:S(2)}) copy-start(bf16[1024,1024]{1,0:T(8,128)(2,1)} %param.9) | copy-start | bytes 6291460
  (28 other events, 101.4 us)
